TPU v7x, 32 devices: a whole 2x2x4 slice. The times are simulated.
32 devices in a mesh: task: 2 (over y), row: 4 (over z), col: 4 (over x, core).
Axes of the slice: x: 2, y: 2, z: 4, core: 2. Of those that a mesh axis runs over, the one named last changes fastest.
Arguments:
- features: bfloat16 [164, 4096], P(None, ('task', 'row', 'col')), parts along dimension 1, may hold values from -6 to 6
- rung_index: int32 [4096], P(('task', 'row', 'col')), parts along dimension 0, may hold values from 0 to 3
- w_first: bfloat16 [164, 512], replicated, may hold values from -0.5 to 0.5
- b_first: float32 [512], replicated, may hold values from -4 to 4
- w_second: bfloat16 [512, 512], replicated, may hold values from -0.25 to 0.25
- b_second: float32 [512], replicated, may hold values from -4 to 4
- w_third: bfloat16 [512, 64], replicated, may hold values from -0.25 to 0.25
- targets: float32 [16, 4096], P(None, ('task', 'row', 'col')), parts along dimension 1, may hold values from -80 to 80
- fidelity_factor: float32 [8, 4], P('task'), parts along dimension 0, may hold values from -4 to 4
- inverse_scale: float32 [2], P('task'), parts along dimension 0, may hold values from 0.02 to 0.1
- noise_var: float32 [2], P('task'), parts along dimension 0, may hold values from 0.3 to 1
Outputs:
- solution: float32 [16, 4096], P(None, ('task', 'row', 'col')), parts along dimension 1
- residual: float32 [16, 4096], P(None, ('task', 'row', 'col')), parts along dimension 1
There are 2 independent parts, one for each index of `task`. A program takes and returns all parts, laid end to end along the dimension named above; an argument that names none is the same for every part. Nothing has to cross between parts.
All inputs are finite; a program needn't handle non-finite values.
Results may differ from a plain program's by a relative error of at most 0.012.
The roundings to bfloat16 on the way count: a program that leaves them out, or rounds other values in their place, can miss the bound.
Values may be sent and summed in bfloat16 or wider, within the bound.
No kernel may reach another device: no remote copies, remote signals or barrier semaphores. Data moves between devices by JAX's collectives and lax.ppermute only.
A program may use at most 64 MiB of HBM per device.

v0:
```python
import jax
import jax.numpy as jnp
from jax import lax
from jax.sharding import PartitionSpec as P

ITERS = 2


def fidelity_matrix(fidelity_factor):
    lower = jnp.tril(fidelity_factor)
    return jnp.dot(lower, lower.T, precision=lax.Precision.HIGHEST) + 0.5 * jnp.eye(
        fidelity_factor.shape[0], dtype=jnp.float32
    )


def left_product(weights, values):
    return lax.dot_general(
        weights, values, (((0,), (0,)), ((), ())), preferred_element_type=jnp.float32
    )


def outer_gram(left_side, right_side):
    return lax.dot_general(
        left_side, right_side, (((1,), (1,)), ((), ())), precision=lax.Precision.HIGHEST
    )


def solve_spd(matrix, right_side):
    return jax.scipy.linalg.cho_solve((jnp.linalg.cholesky(matrix), True), right_side)


def block_size(total_count, largest):
    chosen = min(total_count, largest)
    while total_count % chosen != 0:
        chosen = chosen - 1
    return chosen


def rung_fidelity(fidelity, rung_value):
    levels = jnp.arange(fidelity.shape[0], dtype=jnp.float32)
    onehot = (rung_value.astype(jnp.float32)[None, :] == levels[:, None]).astype(jnp.float32)
    return jnp.dot(fidelity, onehot, precision=lax.Precision.HIGHEST)


def kernel_image(embedding, squares, rung_value, col_fidelity, inverse_scale, direction):
    count = embedding.shape[1]
    row_block = block_size(count, 2048)
    col_block = block_size(count, 2048)
    levels = jnp.arange(col_fidelity.shape[0], dtype=jnp.float32)

    def one_row_block(block_number):
        first_row = block_number * row_block
        rows_embedding = lax.dynamic_slice_in_dim(embedding, first_row, row_block, 1)
        rows_squares = lax.dynamic_slice_in_dim(squares, first_row, row_block, 0)
        rows_rung = lax.dynamic_slice_in_dim(rung_value, first_row, row_block, 0)
        rows_match = rows_rung.astype(jnp.float32)[:, None] == levels[None, :]

        def one_col_block(running, column_number):
            first_col = column_number * col_block
            cols_embedding = lax.dynamic_slice_in_dim(embedding, first_col, col_block, 1)
            cols_squares = lax.dynamic_slice_in_dim(squares, first_col, col_block, 0)
            cols_fidelity = lax.dynamic_slice_in_dim(col_fidelity, first_col, col_block, 1)
            cols_direction = lax.dynamic_slice_in_dim(direction, first_col, col_block, 1)
            inner = left_product(rows_embedding, cols_embedding)
            distance = rows_squares[:, None] + cols_squares[None, :] - 2.0 * inner
            tile_fidelity = cols_fidelity[0][None, :]
            for level in range(1, col_fidelity.shape[0]):
                tile_fidelity = jnp.where(
                    rows_match[:, level : level + 1], cols_fidelity[level][None, :], tile_fidelity
                )
            kernel = jnp.exp(-inverse_scale[0] * distance) * tile_fidelity
            contribution = lax.dot_general(
                cols_direction, kernel, (((1,), (1,)), ((), ())), precision=lax.Precision.HIGHEST
            )
            return (running + contribution, None)

        start_value = jnp.zeros((direction.shape[0], row_block), jnp.float32)
        result, unused = lax.scan(
            one_col_block, start_value, jnp.arange(count // col_block, dtype=jnp.int32)
        )
        return result

    stacked = lax.map(one_row_block, jnp.arange(count // row_block, dtype=jnp.int32))
    return jnp.transpose(stacked, (1, 0, 2)).reshape(direction.shape[0], count)


def on_device(
    features,
    rung_index,
    w_first,
    b_first,
    w_second,
    b_second,
    w_third,
    targets,
    fidelity_factor,
    inverse_scale,
    noise_var,
):
    fidelity = fidelity_matrix(fidelity_factor)
    hidden_one = jax.nn.silu(left_product(w_first, features) + b_first[:, None]).astype(
        jnp.bfloat16
    )
    hidden_two = jax.nn.silu(left_product(w_second, hidden_one) + b_second[:, None]).astype(
        jnp.bfloat16
    )
    embedding = left_product(w_third, hidden_two).astype(jnp.bfloat16)
    rung_value = rung_index.astype(jnp.float32).astype(jnp.bfloat16)
    own_count = targets.shape[1]
    own_first = (lax.axis_index("row") * lax.axis_size("col") + lax.axis_index("col")) * own_count
    all_embedding = lax.all_gather(embedding, ("row", "col"), axis=1, tiled=True)
    all_rung = lax.all_gather(rung_value, ("row", "col"), axis=0, tiled=True)
    all_targets = lax.all_gather(targets, ("row", "col"), axis=1, tiled=True)
    squares = jnp.sum(jnp.square(all_embedding.astype(jnp.float32)), axis=0)
    col_fidelity = rung_fidelity(fidelity, all_rung)
    solution = jnp.zeros_like(all_targets)
    residual = all_targets
    direction = all_targets
    gram = outer_gram(residual, residual)
    for iteration in range(ITERS):
        image = (
            kernel_image(all_embedding, squares, all_rung, col_fidelity, inverse_scale, direction)
            + noise_var[0] * direction
        )
        curvature = outer_gram(direction, image)
        step_matrix = solve_spd(curvature, gram)
        solution = solution + jnp.dot(step_matrix.T, direction, precision=lax.Precision.HIGHEST)
        residual = residual - jnp.dot(step_matrix.T, image, precision=lax.Precision.HIGHEST)
        if iteration + 1 < ITERS:
            new_gram = outer_gram(residual, residual)
            update_matrix = solve_spd(gram, new_gram)
            direction = residual + jnp.dot(
                update_matrix.T, direction, precision=lax.Precision.HIGHEST
            )
            gram = new_gram
    own_solution = lax.dynamic_slice_in_dim(solution, own_first, own_count, 1)
    own_residual = lax.dynamic_slice_in_dim(residual, own_first, own_count, 1)
    return (own_solution, own_residual)


def solution(mesh):
    placed = (
        P(None, ("task", "row", "col")),
        P(("task", "row", "col")),
        P(),
        P(),
        P(),
        P(),
        P(),
        P(None, ("task", "row", "col")),
        P("task", None),
        P("task"),
        P("task"),
    )
    return jax.shard_map(
        on_device,
        mesh=mesh,
        in_specs=placed,
        out_specs=(P(None, ("task", "row", "col")), P(None, ("task", "row", "col"))),
        check_vma=False,
    )
```

profile of v0, /device:TPU:0, one launch (start us, length us, event | category | flops | bytes accessed | tf_op | source)
XLA Modules:
  0.0 122.0 jit_solution(9418712131245514869)
XLA Ops:
  0.6 0.0 copy-start
  0.6 0.7 convert_bitcast_fusion
  1.4 23.1 %all-gather = bf16[16,1,128]{2,1,0:T(2,128)(2,1)S(1)} all-gather(bf16[1,1,128]{2,1,0:T(2,128)(2,1)S(1)} %convert_bitcast_fusion), channel_id=1, replica_groups=mesh['task'=2,'row'=4,'col'=4] {'row','col'}, dimensions={0}, use_global_device_ids=true | all-gather | bytes 4352 | tf_op jit(solution)/shard_map/all_gather | solution.py:112
  24.5 0.9 convolution_add_fusion.4
  25.3 0.2 fusion.5
  25.6 0.1 slice_reduce_fusion.2
  25.7 1.3 %multiply_convert_fusion.1 = bf16[512,128]{1,0:T(8,128)(2,1)S(1)} fusion(bf16[164,512]{1,0:T(8,128)(2,1)} %param.16, bf16[164,128]{1,0:T(8,128)(2,1)} %param.14, f32[512]{0:T(512)} %param.17), kind=kOutput, calls=%fused_computation.14 | convolution fusion | flops 21889024 | bytes 343040 | tf_op jit(solution)/shard_map/dot_general | solution.py:17
  26.9 1.4 %fusion.2 = bf16[64,128]{1,0:T(8,128)(2,1)S(1)} fusion(bf16[512,64]{0,1:T(8,128)(2,1)} %param.20, bf16[512,128]{1,0:T(8,128)(2,1)S(1)} %multiply_convert_fusion.1, bf16[512,512]{1,0:T(8,128)(2,1)S(1)} %copy-done, f32[512]{0:T(512)} %param.19), kind=kOutput, calls=%fused_computation.10 | convolution fusion | flops 75898880 | bytes 739328 | tf_op jit(solution)/shard_map/dot_general | solution.py:17
  28.3 18.2 %all_gather.9 = bf16[64,2048]{1,0:T(8,128)(2,1)S(1)} all-gather(bf16[64,128]{1,0:T(8,128)(2,1)S(1)} %fusion.2), channel_id=1, replica_groups=mesh['task'=2,'row'=4,'col'=4] {'row','col'}, dimensions={1}, use_global_device_ids=true | all-gather | bytes 278528 | tf_op jit(solution)/shard_map/all_gather | solution.py:111
  46.4 0.1 multiply_reduce_fusion
  47.2 0.0 copy-start.2
  47.2 6.6 %select_multiply_fusion = f32[2048,2048]{1,0:T(8,128)S(1)} fusion(bf16[64,2048]{1,0:T(8,128)(2,1)S(1)} %all_gather.9, f32[2048]{0:T(1024)S(1)} %bitcast.95, f32[2048]{0:T(1024)S(1)} %bitcast.96, f32[2048]{0:T(1024)S(1)} %bitcast.97, f32[2048]{0:T(1024)S(1)} %bitcast.94, f32[2048]{0:T(1024)S(1)} %multiply_reduce_fusion, f32[]{:T(128)} %bitcast, ...), kind=kOutput, calls=%fused_computation | convolution fusion | flops 570425344 | bytes 17086468 | tf_op jit(solution)/shard_map/while/body/eval_jaxpr/while/body/eval_jaxpr/dot_general | solution.py:17
  53.8 0.0 copy-done.2
  53.8 19.3 %all_gather.11 = f32[16,2048]{1,0:T(8,128)S(1)} all-gather(f32[16,128]{1,0:T(8,128)S(1)} %copy-done.2), channel_id=1, replica_groups=mesh['task'=2,'row'=4,'col'=4] {'row','col'}, dimensions={1}, use_global_device_ids=true | all-gather | bytes 139264 | tf_op jit(solution)/shard_map/all_gather | solution.py:113
  73.7 0.0 copy-done.1
  73.8 14.1 %fusion = f32[16,2048]{1,0:T(8,128)S(1)} fusion(f32[2048,2048]{1,0:T(8,128)S(1)} %select_multiply_fusion, f32[16,2048]{1,0:T(8,128)S(1)} %all_gather.11, f32[]{:T(128)} %bitcast.89), kind=kOutput, calls=%fused_computation.5 | convolution fusion | flops 805371904 | bytes 17039364 | tf_op jit(solution)/shard_map/while/body/eval_jaxpr/while/body/eval_jaxpr/dot_general | solution.py:72
  87.9 0.2 fusion.29
  88.1 0.1 copy.22
  88.2 1.5 %cholesky.59 = f32[16,16]{1,0:T(8,128)S(1)} custom-call(f32[16,16]{1,0:T(8,128)S(1)} %add_multiply_fusion), custom_call_target="Cholesky" | custom-call | tf_op jit(solution)/shard_map/jit(cholesky)/cholesky | solution.py:29
  89.8 0.6 compare_reduce_fusion.2
  90.4 0.6 fusion.7
  91.1 1.2 %custom-call.9 = f32[1,16,16]{1,2,0:T(8,128)S(1)} custom-call(f32[1,16,16]{2,1,0:T(8,128)S(1)} %fusion.7), custom_call_target="InvertDiagBlocksLowerTriangular" | custom-call | tf_op jit(solution)/shard_map/jit(_cho_solve)/triangular_solve | solution.py:29
  92.3 0.2 fusion.30
  92.5 0.3 fusion.22
  92.8 0.1 fusion.20
  93.0 0.3 convolution_subtract_fusion
  93.3 0.4 fusion.32
  93.7 0.1 copy.23
  93.8 1.5 %cholesky.70 = f32[16,16]{1,0:T(8,128)S(1)} custom-call(f32[16,16]{1,0:T(8,128)S(1)} %fusion.19), custom_call_target="Cholesky" | custom-call | tf_op jit(solution)/shard_map/jit(cholesky)/cholesky | solution.py:29
  95.4 0.6 compare_reduce_fusion.1
  96.0 0.6 fusion.8
  96.7 1.2 %custom-call.10 = f32[1,16,16]{1,2,0:T(8,128)S(1)} custom-call(f32[1,16,16]{2,1,0:T(8,128)S(1)} %fusion.8), custom_call_target="InvertDiagBlocksLowerTriangular" | custom-call | tf_op jit(solution)/shard_map/jit(_cho_solve)/triangular_solve | solution.py:29
  97.9 0.2 fusion.17
  98.1 0.1 fusion.15
  98.2 0.3 convolution_add_fusion
  98.6 17.1 %convolution_add_fusion.1 = f32[16,2048]{1,0:T(8,128)S(1)} fusion(f32[16,2048]{1,0:T(8,128)S(1)} %convolution_add_fusion, f32[2048,2048]{1,0:T(8,128)} %copy-done.1, f32[]{:T(128)} %bitcast.90), kind=kOutput, calls=%fused_computation.3 | convolution fusion | flops 805371904 | bytes 17039364 | tf_op jit(solution)/shard_map/while/body/eval_jaxpr/while/body/eval_jaxpr/dot_general | solution.py:72
  115.7 0.2 fusion.33
  115.9 0.1 copy.24
  116.0 1.5 %cholesky.81 = f32[16,16]{1,0:T(8,128)S(1)} custom-call(f32[16,16]{1,0:T(8,128)S(1)} %fusion.14), custom_call_target="Cholesky" | custom-call | tf_op jit(solution)/shard_map/jit(cholesky)/cholesky | solution.py:29
  117.5 0.6 compare_reduce_fusion
  118.2 0.6 fusion.9
  118.9 1.2 %custom-call.11 = f32[1,16,16]{1,2,0:T(8,128)S(1)} custom-call(f32[1,16,16]{2,1,0:T(8,128)S(1)} %fusion.9), custom_call_target="InvertDiagBlocksLowerTriangular" | custom-call | tf_op jit(solution)/shard_map/jit(_cho_solve)/triangular_solve | solution.py:29
  120.1 0.2 fusion.12
  120.3 0.1 fusion.10
  120.4 0.3 fusion.34
  120.8 0.3 fusion.35
  121.1 0.3 fusion.31
  121.4 0.6 dynamic-slice_subtract_fusion
  (11 shorter events, 0.2 us)
Async XLA Ops:
  0.6 26.3 %copy-start = (bf16[512,512]{1,0:T(8,128)(2,1)S(1)}, bf16[512,512]{1,0:T(8,128)(2,1)}, u32[]{:S(2)}) copy-start(bf16[512,512]{1,0:T(8,128)(2,1)} %param.18) | copy-start | bytes 1572868
  47.2 6.6 %copy-start.2 = (f32[16,128]{1,0:T(8,128)S(1)}, f32[16,128]{1,0:T(8,128)}, u32[]{:S(2)}) copy-start(f32[16,128]{1,0:T(8,128)} %param.21) | copy-start | bytes 24580
  53.8 20.0 %copy-start.1 = (f32[2048,2048]{1,0:T(8,128)}, f32[2048,2048]{1,0:T(8,128)S(1)}, u32[]{:S(2)}) copy-start(f32[2048,2048]{1,0:T(8,128)S(1)} %select_multiply_fusion) | copy-start | bytes 50331652
where the time goes:
time: 122 us
  blocking collectives  60.5 us (50%)
  matrix products  45.3 us (37%)
  other arithmetic  13.7 us (11%)
  between operations  2.14 us (2%)
    dot_general x2, matrix products, one_col_block(): lax.dot_general(cols_direction, kernel, (((1,), (1,)), ((), ())), precisi...  31.2 us
    all_gather x1, blocking collectives, on_device(): all_rung = lax.all_gather(rung_value, ('row', 'col'), axis=0, tiled=True)  23.1 us
    all_gather x1, blocking collectives, on_device(): all_targets = lax.all_gather(targets, ('row', 'col'), axis=1, tiled=True)  19.3 us
    all_gather x1, blocking collectives, on_device(): lax.all_gather(embedding, ('row', 'col'), axis=1, tiled=True)  18.2 us
    dot_general x3, matrix products, left_product(): lax.dot_general(weights, values, (((0,), (0,)), ((), ())), preferred_elem...  9.19 us
    another operation x9, other arithmetic, solve_spd(): jnp.linalg.cholesky(matrix)  6.57 us
    another operation x6, other arithmetic, solve_spd(): jax.scipy.linalg.cho_solve((jnp.linalg.cholesky(matrix), True), right_side)  5.63 us

commit v1 on v0

--- a/solution.py
+++ b/solution.py
@@ -4,6 +4,28 @@
 from jax.sharding import PartitionSpec as P
 
 ITERS = 2
+
+
+def joined_along(blocks, dim):
+    blocks = jnp.moveaxis(blocks, 0, dim)
+    lengths = blocks.shape
+    return blocks.reshape(*lengths[:dim], lengths[dim] * lengths[dim + 1], *lengths[dim + 2 :])
+
+
+def grow_blocks(value, axis):
+    size = lax.axis_size(axis)
+    parts = value[None]
+    for level in range(size.bit_length() - 1):
+        bit = 1 << level
+        other = lax.ppermute(parts, axis, [(i, i ^ bit) for i in range(size)])
+        both = jnp.stack([parts, other])
+        upper = lax.axis_index(axis) >> level & 1
+        parts = jnp.where(upper == 0, both, both[::-1]).reshape(-1, *value.shape)
+    return parts
+
+
+def collect(x, axis, dim):
+    return joined_along(grow_blocks(x, axis), dim)
 
 
 def fidelity_matrix(fidelity_factor):
@@ -110,7 +132,7 @@
     own_first = (lax.axis_index("row") * lax.axis_size("col") + lax.axis_index("col")) * own_count
     all_embedding = lax.all_gather(embedding, ("row", "col"), axis=1, tiled=True)
     all_rung = lax.all_gather(rung_value, ("row", "col"), axis=0, tiled=True)
-    all_targets = lax.all_gather(targets, ("row", "col"), axis=1, tiled=True)
+    all_targets = collect(targets, ("row", "col"), 1)
     squares = jnp.sum(jnp.square(all_embedding.astype(jnp.float32)), axis=0)
     col_fidelity = rung_fidelity(fidelity, all_rung)
     solution = jnp.zeros_like(all_targets)

time: 122 us -> 118 us (0.967)
  blocking collectives: 60.5 us -> 40.8 us
  matrix products: 45.3 us -> 52.2 us
  waiting for transfers between devices: 0 us -> 5.15 us
  starting transfers between devices: 0 us -> 2.38 us
    all_gather x1 -> x0, blocking collectives: 19.3 us -> none  [on_device(): all_targets = lax.all_gather(targets, ('row', 'col'), axis=1, tiled=True)]
    ppermute x0 -> x4, waiting for transfers between devices: none -> 5.15 us  [grow_blocks(): other = lax.ppermute(parts, axis, [(i, i ^ bit) for i in range(size)])]
    dot_general x3, matrix products: 9.19 us -> 13.1 us  [left_product(): lax.dot_general(weights, values, (((0,), (0,)), ((), ())), preferred_elem...]
    dot_general x2, matrix products: 31.2 us -> 34.4 us  [one_col_block(): lax.dot_general(cols_direction, kernel, (((1,), (1,)), ((), ())), precisi...]
    ppermute x0 -> x4, starting transfers between devices: none -> 2.38 us  [grow_blocks(): other = lax.ppermute(parts, axis, [(i, i ^ bit) for i in range(size)])]
  transfers between devices with their start and end apart: 0 -> 4, of which waited for: 0 -> 2; matrix products, arithmetic and copies ran while one was open for 0% -> 13% of each run, Pallas kernels for 0% -> 0%
where the time goes in v1:
time: 118 us; the launch traced here: 117 us
  matrix products  52.2 us (44%)
  blocking collectives  40.8 us (35%)
  other arithmetic  14.3 us (12%)
  waiting for transfers between devices  5.15 us (4%)
  starting transfers between devices  2.38 us (2%)
  between operations  2.14 us (2%)
    dot_general x2, matrix products, one_col_block(): lax.dot_general(cols_direction, kernel, (((1,), (1,)), ((), ())), precisi...  34.4 us
    all_gather x1, blocking collectives, on_device(): all_rung = lax.all_gather(rung_value, ('row', 'col'), axis=0, tiled=True)  22.7 us
    all_gather x1, blocking collectives, on_device(): lax.all_gather(embedding, ('row', 'col'), axis=1, tiled=True)  18.2 us
    dot_general x3, matrix products, left_product(): lax.dot_general(weights, values, (((0,), (0,)), ((), ())), preferred_elem...  13.1 us
    another operation x9, other arithmetic, solve_spd(): jnp.linalg.cholesky(matrix)  6.51 us
    another operation x6, other arithmetic, solve_spd(): jax.scipy.linalg.cho_solve((jnp.linalg.cholesky(matrix), True), right_side)  5.63 us
    ppermute x4, waiting for transfers between devices, grow_blocks(): other = lax.ppermute(parts, axis, [(i, i ^ bit) for i in range(size)])  5.15 us
    ppermute x4, starting transfers between devices, grow_blocks(): other = lax.ppermute(parts, axis, [(i, i ^ bit) for i in range(size)])  2.38 us
  transfers between devices with their start and end apart: 4, of which 2 were waited for; matrix products, arithmetic and copies ran while one was open for 13% of the time, Pallas kernels for 0%

profile of v1, /device:TPU:0, one launch (start us, length us, event | category | flops | bytes accessed | tf_op | source)
XLA Modules:
  0.0 117.4 jit_solution(16731224381298234991)
XLA Ops:
  0.6 0.6 collective-permute-start
  1.2 0.7 convert_bitcast_fusion
  1.9 0.9 convolution_add_fusion.5
  2.7 22.7 %all-gather = bf16[16,1,128]{2,1,0:T(2,128)(2,1)S(1)} all-gather(bf16[1,1,128]{2,1,0:T(2,128)(2,1)S(1)} %convert_bitcast_fusion), channel_id=1, replica_groups=mesh['task'=2,'row'=4,'col'=4] {'row','col'}, dimensions={0}, use_global_device_ids=true | all-gather | bytes 4352 | tf_op jit(solution)/shard_map/all_gather | solution.py:134
  25.4 0.2 fusion.14
  25.6 1.3 %multiply_convert_fusion.1 = bf16[512,128]{1,0:T(8,128)(2,1)S(1)} fusion(bf16[164,512]{1,0:T(8,128)(2,1)} %param.16, bf16[164,128]{1,0:T(8,128)(2,1)} %param.14, f32[512]{0:T(512)} %param.17), kind=kOutput, calls=%fused_computation.14 | convolution fusion | flops 21889024 | bytes 343040 | tf_op jit(solution)/shard_map/dot_general | solution.py:39
  26.9 1.3 %fusion.1 = bf16[64,128]{1,0:T(8,128)(2,1)S(1)} fusion(bf16[512,64]{0,1:T(8,128)(2,1)} %param.20, bf16[512,128]{1,0:T(8,128)(2,1)S(1)} %multiply_convert_fusion.1, bf16[512,512]{1,0:T(8,128)(2,1)S(1)} %copy-done, f32[512]{0:T(512)} %param.19), kind=kOutput, calls=%fused_computation.9 | convolution fusion | flops 75898880 | bytes 739328 | tf_op jit(solution)/shard_map/dot_general | solution.py:39
  28.3 18.2 %all_gather.6 = bf16[64,2048]{1,0:T(8,128)(2,1)S(1)} all-gather(bf16[64,128]{1,0:T(8,128)(2,1)S(1)} %fusion.1), channel_id=1, replica_groups=mesh['task'=2,'row'=4,'col'=4] {'row','col'}, dimensions={1}, use_global_device_ids=true | all-gather | bytes 278528 | tf_op jit(solution)/shard_map/all_gather | solution.py:133
  46.4 0.7 pad_maximum_fusion.3
  47.1 1.7 %collective-permute-start.1 = (f32[2,16,128]{2,1,0:T(8,128)S(1)}, f32[2,16,128]{2,1,0:T(8,128)S(1)}, u32[]{:S(2)}, u32[]{:S(2)}) collective-permute-start(f32[2,16,128]{2,1,0:T(8,128)S(1)} %get-tuple-element.137), channel_id=1, source_target_pairs={{0,2},{1,3},{2,0},{3,1},{4,6},{5,7},{6,4},{7,5},{8,10},{9,11},{10,... | collective-permute-start | bytes 49160 | tf_op jit(solution)/shard_map/ppermute | solution.py:20
  48.9 2.0 %collective-permute-done.1 = f32[2,16,128]{2,1,0:T(8,128)S(1)} collective-permute-done((f32[2,16,128]{2,1,0:T(8,128)S(1)}, f32[2,16,128]{2,1,0:T(8,128)S(1)}, u32[]{:S(2)}, u32[]{:S(2)}) %collective-permute-start.1) | collective-permute-done | bytes 16416 | tf_op jit(solution)/shard_map/ppermute | solution.py:20
  51.0 0.1 slice_reduce_fusion.2
  51.7 3.2 %collective-permute-done.2 = f32[4,16,128]{2,1,0:T(8,128)S(1)} collective-permute-done((f32[4,16,128]{2,1,0:T(8,128)S(1)}, f32[4,16,128]{2,1,0:T(8,128)S(1)}, u32[]{:S(2)}, u32[]{:S(2)}) %collective-permute-start.2) | collective-permute-done | bytes 32800 | tf_op jit(solution)/shard_map/ppermute | solution.py:20
  54.9 0.1 collective-permute-start.3
  55.0 10.5 %select_multiply_fusion = f32[2048,2048]{1,0:T(8,128)} fusion(bf16[64,2048]{1,0:T(8,128)(2,1)S(1)} %all_gather.6, f32[2048]{0:T(1024)S(1)} %bitcast.136, f32[2048]{0:T(1024)S(1)} %bitcast.137, f32[2048]{0:T(1024)S(1)} %bitcast.138, f32[2048]{0:T(1024)S(1)} %bitcast.135, f32[2048]{0:T(1024)S(1)} %multiply_reduce_fusion, f32[]{:T(128)} %bitcast.14, ...), kind=kOutput, calls=%fused_computation | convolution fusion | flops 570425344 | bytes 17086468 | tf_op jit(solution)/shard_map/while/body/eval_jaxpr/while/body/eval_jaxpr/dot_general | solution.py:39
  66.2 0.2 convolution_bitcast_fusion
  66.4 0.1 copy.26
  66.5 17.2 %convolution_add_fusion.2 = f32[16,2048]{1,0:T(8,128)S(1)} fusion(f32[2048,2048]{1,0:T(8,128)} %select_multiply_fusion, f32[16,2,8,128]{3,2,1,0:T(8,128)S(1)} %bitcast.118, f32[]{:T(128)} %bitcast.115), kind=kOutput, calls=%fused_computation.4 | convolution fusion | flops 805371904 | bytes 17039364 | tf_op jit(solution)/shard_map/while/body/eval_jaxpr/while/body/eval_jaxpr/dot_general | solution.py:94
  83.7 0.2 fusion.5
  83.9 0.1 copy.25
  84.0 1.5 %cholesky.59 = f32[16,16]{1,0:T(8,128)S(1)} custom-call(f32[16,16]{1,0:T(8,128)S(1)} %fusion.35), custom_call_target="Cholesky" | custom-call | tf_op jit(solution)/shard_map/jit(cholesky)/cholesky | solution.py:51
  85.5 0.6 compare_reduce_fusion.2
  86.2 0.6 fusion.18
  86.8 1.2 %custom-call.9 = f32[1,16,16]{1,2,0:T(8,128)S(1)} custom-call(f32[1,16,16]{2,1,0:T(8,128)S(1)} %fusion.18), custom_call_target="InvertDiagBlocksLowerTriangular" | custom-call | tf_op jit(solution)/shard_map/jit(_cho_solve)/triangular_solve | solution.py:51
  88.1 0.2 fusion.33
  88.3 0.1 fusion.31
  88.4 0.3 convolution_subtract_fusion
  88.8 0.3 fusion.3
  89.1 1.4 %cholesky.70 = f32[16,16]{1,0:T(8,128)S(1)} custom-call(f32[16,16]{1,0:T(8,128)S(1)} %fusion.30), custom_call_target="Cholesky" | custom-call | tf_op jit(solution)/shard_map/jit(cholesky)/cholesky | solution.py:51
  90.6 0.6 compare_reduce_fusion.1
  91.2 0.6 fusion.19
  91.9 1.2 %custom-call.10 = f32[1,16,16]{1,2,0:T(8,128)S(1)} custom-call(f32[1,16,16]{2,1,0:T(8,128)S(1)} %fusion.19), custom_call_target="InvertDiagBlocksLowerTriangular" | custom-call | tf_op jit(solution)/shard_map/jit(_cho_solve)/triangular_solve | solution.py:51
  93.1 0.2 fusion.41
  93.3 0.3 fusion.28
  93.6 0.1 fusion.26
  93.7 0.3 convolution_add_fusion
  94.1 17.3 %convolution_add_fusion.1 = f32[16,2048]{1,0:T(8,128)S(1)} fusion(f32[16,2048]{1,0:T(8,128)S(1)} %convolution_add_fusion, f32[2048,2048]{1,0:T(8,128)} %select_multiply_fusion, f32[]{:T(128)} %bitcast.116), kind=kOutput, calls=%fused_computation.3 | convolution fusion | flops 805371904 | bytes 17039364 | tf_op jit(solution)/shard_map/while/body/eval_jaxpr/while/body/eval_jaxpr/dot_general | solution.py:94
  111.3 0.2 fusion.42
  111.6 0.1 copy.27
  111.7 1.5 %cholesky.81 = f32[16,16]{1,0:T(8,128)S(1)} custom-call(f32[16,16]{1,0:T(8,128)S(1)} %fusion.25), custom_call_target="Cholesky" | custom-call | tf_op jit(solution)/shard_map/jit(cholesky)/cholesky | solution.py:51
  113.2 0.6 compare_reduce_fusion
  113.9 0.6 fusion.20
  114.5 1.2 %custom-call.11 = f32[1,16,16]{1,2,0:T(8,128)S(1)} custom-call(f32[1,16,16]{2,1,0:T(8,128)S(1)} %fusion.20), custom_call_target="InvertDiagBlocksLowerTriangular" | custom-call | tf_op jit(solution)/shard_map/jit(_cho_solve)/triangular_solve | solution.py:51
  115.8 0.2 fusion.23
  116.0 0.1 fusion.21
  116.1 0.3 fusion.44
  116.4 0.3 fusion.43
  116.8 0.6 dynamic-slice_subtract_fusion
  (22 shorter events, 0.4 us)
Async XLA Ops:
  0.6 26.3 %copy-start = (bf16[512,512]{1,0:T(8,128)(2,1)S(1)}, bf16[512,512]{1,0:T(8,128)(2,1)}, u32[]{:S(2)}) copy-start(bf16[512,512]{1,0:T(8,128)(2,1)} %param.18) | copy-start | bytes 1572868
  0.6 45.8 %collective-permute-start = (f32[1,16,128]{2,1,0:T(8,128)}, f32[1,16,128]{2,1,0:T(8,128)S(1)}, u32[]{:S(2)}, u32[]{:S(2)}) collective-permute-start(f32[1,16,128]{2,1,0:T(8,128)} %bitcast.132), channel_id=1, source_target_pairs={{0,1},{1,0},{2,3},{3,2},{4,5},{5,4},{6,7},{7,6},{8,9},{9,8},{10,11... | collective-permute-start | bytes 24584 | tf_op jit(solution)/shard_map/ppermute | solution.py:20
  47.1 3.7 %collective-permute-start.1 = (f32[2,16,128]{2,1,0:T(8,128)S(1)}, f32[2,16,128]{2,1,0:T(8,128)S(1)}, u32[]{:S(2)}, u32[]{:S(2)}) collective-permute-start(f32[2,16,128]{2,1,0:T(8,128)S(1)} %get-tuple-element.137), channel_id=1, source_target_pairs={{0,2},{1,3},{2,0},{3,1},{4,6},{5,7},{6,4},{7,5},{8,10},{9,11},{10,... | collective-permute-start | bytes 49160 | tf_op jit(solution)/shard_map/ppermute | solution.py:20
  50.9 4.0 %collective-permute-start.2 = (f32[4,16,128]{2,1,0:T(8,128)S(1)}, f32[4,16,128]{2,1,0:T(8,128)S(1)}, u32[]{:S(2)}, u32[]{:S(2)}) collective-permute-start(f32[4,16,128]{2,1,0:T(8,128)S(1)} %bitcast.125), channel_id=1, source_target_pairs={{0,4},{1,5},{2,6},{3,7},{4,0},{5,1},{6,2},{7,3},{8,12},{9,13},{10,... | collective-permute-start | bytes 98312 | tf_op jit(solution)/shard_map/ppermute | solution.py:20
  54.9 11.3 %collective-permute-start.3 = (f32[8,16,128]{2,1,0:T(8,128)S(1)}, f32[8,16,128]{2,1,0:T(8,128)S(1)}, u32[]{:S(2)}, u32[]{:S(2)}) collective-permute-start(f32[8,16,128]{2,1,0:T(8,128)S(1)} %bitcast.123), channel_id=1, source_target_pairs={{0,8},{1,9},{2,10},{3,11},{4,12},{5,13},{6,14},{7,15},{8,0},{9,1},... | collective-permute-start | bytes 196616 | tf_op jit(solution)/shard_map/ppermute | solution.py:20
